TPU v7x, 32 devices: a whole 2x2x4 slice. The times are simulated.
32 devices in a mesh: tm: 8 (over z, y), col: 4 (over x, core).
Axes of the slice: x: 2, y: 2, z: 4, core: 2. Of those that a mesh axis runs over, the one named last changes fastest.
Arguments:
- observed: bfloat16 [16, 128, 512], P('tm', None, 'col'), may hold values from -6 to 6
- input_gain: float32 [512], P('col'), may hold values from 0.03 to 0.3
- persist: float32 [16, 512], P('tm', 'col'), may hold values from 0.5 to 1, as said below
- coupling: bfloat16 [16, 512, 512], P('tm', None, 'col'), may hold values from -0.02734375 to 0.02734375
- pattern: int32 [8, 8], replicated, may hold values 0 or 1
Outputs:
- filtered: float32 [16, 128, 512], P('tm', None, 'col')
- smoothed: float32 [16, 128, 512], P('tm', None, 'col')
Inputs may be any that keep to these rules, and one draw needn't show every extreme that they name: `persist`: persistence of each state component at each step.
All inputs are finite; a program needn't handle non-finite values.
Results may differ from a plain program's by a relative error of at most 0.0003.
Values may be sent and summed in bfloat16 or wider, within the bound.
No kernel may reach another device: no remote copies, remote signals or barrier semaphores. Data moves between devices by JAX's collectives and lax.ppermute only.
A program may use at most 64 MiB of HBM per device.

v0:
```python
import jax
import jax.numpy as jnp
from jax import lax
from jax.sharding import PartitionSpec as P


def passed_along(shard, axis, by):
    length = lax.axis_size(axis)
    pairs = [(i, i + by) for i in range(length) if 0 <= i + by < length]
    return lax.ppermute(shard, axis, pairs)


def split_dot(state, weights, transposed):
    high = state.astype(jnp.bfloat16)
    low = (state - high.astype(jnp.float32)).astype(jnp.bfloat16)
    both = jnp.concatenate([high, low], axis=0)
    contract = 1 if transposed else 0
    prod = lax.dot_general(
        both, weights, (((1,), (contract,)), ((), ())), preferred_element_type=jnp.float32
    )
    rows = state.shape[0]
    return prod[:rows] + prod[rows:]


def local(observed, input_gain, persist, coupling, pattern):
    step_count = observed.shape[0]
    state_width = coupling.shape[1]
    block_count = pattern.shape[0]
    block_size = state_width // block_count
    time_groups = lax.axis_size("tm")
    full_coupling = lax.all_gather(coupling, "col", axis=2, tiled=True)
    small = jnp.concatenate([persist, input_gain[None]], axis=0)
    small = lax.all_gather(small, "col", axis=1, tiled=True)
    diag = small[:step_count]
    gain = small[step_count]
    seen = lax.all_to_all(observed, "col", split_axis=1, concat_axis=2, tiled=True)
    mask = jnp.broadcast_to(
        pattern.astype(jnp.bfloat16)[:, None, :, None],
        (block_count, block_size, block_count, block_size),
    ).reshape(state_width, state_width)
    weights = full_coupling * mask[None]
    driven = gain[None, None, :] * seen.astype(jnp.float32)

    def forward(x):
        out = []
        for k in range(step_count):
            x = split_dot(x, weights[k], False) + x * diag[k][None] + driven[k]
            out.append(x)
        return out

    def backward(e):
        out = [None] * step_count
        out[step_count - 1] = e
        for k in range(step_count - 1, -1, -1):
            w = e + driven[k]
            e = split_dot(w, weights[k], True) + w * diag[k][None]
            if k > 0:
                out[k - 1] = e
        return (out, e)

    def stage(carry):
        x_in, e_in = carry
        xs = forward(x_in)
        _, e_out = backward(e_in)
        return (passed_along(xs[-1], "tm", 1), passed_along(e_out, "tm", -1))

    zeros = jnp.zeros(driven.shape[1:], jnp.float32)
    carry = (zeros, zeros)
    if time_groups <= 8:
        for _ in range(time_groups - 1):
            carry = stage(carry)
    else:
        carry = lax.fori_loop(0, time_groups - 1, lambda _, c: stage(c), carry)
    x_in, e_in = carry
    xs = forward(x_in)
    es, _ = backward(e_in)
    filtered = jnp.stack(xs)
    smoothed = jnp.stack([x + e for x, e in zip(xs, es)])
    both = jnp.stack([filtered, smoothed])
    both = lax.all_to_all(both, "col", split_axis=3, concat_axis=2, tiled=True)
    return (both[0], both[1])


def solution(mesh):
    return jax.shard_map(
        local,
        mesh=mesh,
        in_specs=(P("tm", None, "col"), P("col"), P("tm", "col"), P("tm", None, "col"), P()),
        out_specs=(P("tm", None, "col"), P("tm", None, "col")),
        check_vma=False,
    )
```

profile of v0, /device:TPU:0, one launch (start us, length us, event | category | flops | bytes accessed | tf_op | source)
XLA Modules:
  0.0 149.8 jit_solution(448652533752614488)
XLA Ops:
  7.2 0.7 all-gather.2.cloned.1.call-update
  8.0 0.7 copy.10
  8.7 4.2 %all-to-all-start = ((bf16[2,128,128]{2,0,1:T(2,128)(2,1)}), bf16[2,128,128]{2,0,1:T(2,128)(2,1)S(1)}, u32[]{:S(2)}, u32[]{:S(2)}) async-start(bf16[2,128,128]{2,0,1:T(2,128)(2,1)} %copy.10), calls=%async_computation | async-start | bytes 131072 | tf_op jit(solution)/shard_map/all_to_all | solution.py:36
  12.9 0.7 copy-done.2
  13.6 5.3 %all_gather.7 = f32[3,512]{1,0:T(4,128)S(1)} all-gather(f32[3,128]{1,0:T(4,128)S(1)} %pad_maximum_fusion.1), channel_id=1, replica_groups=mesh['tm'=8,'col'=4] {'col'}, dimensions={1}, use_global_device_ids=true | all-gather | bytes 7680 | tf_op jit(solution)/shard_map/all_gather | solution.py:33
  18.9 0.7 copy-done.1
  19.8 0.6 mul.82
  20.6 8.5 %all-gather.2.cloned.1.call-done = bf16[2,512,512]{2,1,0:T(8,128)(2,1)} async-done(((bf16[2,512,128]{2,1,0:T(8,128)(2,1)}), bf16[2,512,512]{2,1,0:T(8,128)(2,1)}) %all-gather.2.cloned.1.call-update) | async-done | bytes 1048592 | tf_op jit(solution)/shard_map/all_gather | solution.py:31
  29.1 1.3 broadcast_multiply_fusion
  30.9 3.4 %collective-permute-start = (f32[32,512]{1,0:T(8,128)S(1)}, f32[32,512]{1,0:T(8,128)S(1)}, u32[]{:S(2)}, u32[]{:S(2)}) collective-permute-start(f32[32,512]{1,0:T(8,128)S(1)} %fusion.53), channel_id=1, source_target_pairs={{0,4},{4,8},{8,12},{12,16},{16,20},{20,24},{24,28},{1,5},{5,9},{9,... | collective-permute-start | bytes 196616 | tf_op jit(solution)/shard_map/ppermute | solution.py:10
  34.3 1.9 %collective-permute-done = f32[32,512]{1,0:T(8,128)S(1)} collective-permute-done((f32[32,512]{1,0:T(8,128)S(1)}, f32[32,512]{1,0:T(8,128)S(1)}, u32[]{:S(2)}, u32[]{:S(2)}) %collective-permute-start) | collective-permute-done | bytes 65568 | tf_op jit(solution)/shard_map/ppermute | solution.py:10
  36.7 4.3 %collective-permute-start.1 = (f32[32,512]{1,0:T(8,128)S(1)}, f32[32,512]{1,0:T(8,128)S(1)}, u32[]{:S(2)}, u32[]{:S(2)}) collective-permute-start(f32[32,512]{1,0:T(8,128)S(1)} %fusion.49), channel_id=1, source_target_pairs={{0,4},{4,8},{8,12},{12,16},{16,20},{20,24},{24,28},{1,5},{5,9},{9,... | collective-permute-start | bytes 196616 | tf_op jit(solution)/shard_map/ppermute | solution.py:10
  40.9 1.9 %collective-permute-done.1 = f32[32,512]{1,0:T(8,128)S(1)} collective-permute-done((f32[32,512]{1,0:T(8,128)S(1)}, f32[32,512]{1,0:T(8,128)S(1)}, u32[]{:S(2)}, u32[]{:S(2)}) %collective-permute-start.1) | collective-permute-done | bytes 65568 | tf_op jit(solution)/shard_map/ppermute | solution.py:10
  43.3 4.3 %collective-permute-start.2 = (f32[32,512]{1,0:T(8,128)S(1)}, f32[32,512]{1,0:T(8,128)S(1)}, u32[]{:S(2)}, u32[]{:S(2)}) collective-permute-start(f32[32,512]{1,0:T(8,128)S(1)} %fusion.45), channel_id=1, source_target_pairs={{0,4},{4,8},{8,12},{12,16},{16,20},{20,24},{24,28},{1,5},{5,9},{9,... | collective-permute-start | bytes 196616 | tf_op jit(solution)/shard_map/ppermute | solution.py:10
  47.6 1.9 %collective-permute-done.2 = f32[32,512]{1,0:T(8,128)S(1)} collective-permute-done((f32[32,512]{1,0:T(8,128)S(1)}, f32[32,512]{1,0:T(8,128)S(1)}, u32[]{:S(2)}, u32[]{:S(2)}) %collective-permute-start.2) | collective-permute-done | bytes 65568 | tf_op jit(solution)/shard_map/ppermute | solution.py:10
  50.0 5.2 %collective-permute-start.3 = (f32[32,512]{1,0:T(8,128)S(1)}, f32[32,512]{1,0:T(8,128)S(1)}, u32[]{:S(2)}, u32[]{:S(2)}) collective-permute-start(f32[32,512]{1,0:T(8,128)S(1)} %fusion.41), channel_id=1, source_target_pairs={{0,4},{4,8},{8,12},{12,16},{16,20},{20,24},{24,28},{1,5},{5,9},{9,... | collective-permute-start | bytes 196616 | tf_op jit(solution)/shard_map/ppermute | solution.py:10
  55.2 1.9 %collective-permute-done.3 = f32[32,512]{1,0:T(8,128)S(1)} collective-permute-done((f32[32,512]{1,0:T(8,128)S(1)}, f32[32,512]{1,0:T(8,128)S(1)}, u32[]{:S(2)}, u32[]{:S(2)}) %collective-permute-start.3) | collective-permute-done | bytes 65568 | tf_op jit(solution)/shard_map/ppermute | solution.py:10
  57.5 5.2 %collective-permute-start.4 = (f32[32,512]{1,0:T(8,128)S(1)}, f32[32,512]{1,0:T(8,128)S(1)}, u32[]{:S(2)}, u32[]{:S(2)}) collective-permute-start(f32[32,512]{1,0:T(8,128)S(1)} %fusion.37), channel_id=1, source_target_pairs={{0,4},{4,8},{8,12},{12,16},{16,20},{20,24},{24,28},{1,5},{5,9},{9,... | collective-permute-start | bytes 196616 | tf_op jit(solution)/shard_map/ppermute | solution.py:10
  62.7 1.9 %collective-permute-done.4 = f32[32,512]{1,0:T(8,128)S(1)} collective-permute-done((f32[32,512]{1,0:T(8,128)S(1)}, f32[32,512]{1,0:T(8,128)S(1)}, u32[]{:S(2)}, u32[]{:S(2)}) %collective-permute-start.4) | collective-permute-done | bytes 65568 | tf_op jit(solution)/shard_map/ppermute | solution.py:10
  65.1 5.2 %collective-permute-start.5 = (f32[32,512]{1,0:T(8,128)S(1)}, f32[32,512]{1,0:T(8,128)S(1)}, u32[]{:S(2)}, u32[]{:S(2)}) collective-permute-start(f32[32,512]{1,0:T(8,128)S(1)} %fusion.33), channel_id=1, source_target_pairs={{0,4},{4,8},{8,12},{12,16},{16,20},{20,24},{24,28},{1,5},{5,9},{9,... | collective-permute-start | bytes 196616 | tf_op jit(solution)/shard_map/ppermute | solution.py:10
  70.2 1.9 %collective-permute-done.5 = f32[32,512]{1,0:T(8,128)S(1)} collective-permute-done((f32[32,512]{1,0:T(8,128)S(1)}, f32[32,512]{1,0:T(8,128)S(1)}, u32[]{:S(2)}, u32[]{:S(2)}) %collective-permute-start.5) | collective-permute-done | bytes 65568 | tf_op jit(solution)/shard_map/ppermute | solution.py:10
  72.6 0.3 fusion.116
  73.2 1.3 collective-permute-start.7
  74.5 6.6 %collective-permute-done.7 = f32[32,512]{1,0:T(8,128)S(1)} collective-permute-done((f32[32,512]{1,0:T(8,128)S(1)}, f32[32,512]{1,0:T(8,128)S(1)}, u32[]{:S(2)}, u32[]{:S(2)}) %collective-permute-start.7) | collective-permute-done | bytes 65568 | tf_op jit(solution)/shard_map/ppermute | solution.py:10
  81.2 0.3 fusion.124
  81.5 0.3 fusion.128
  81.8 1.3 collective-permute-start.8
  83.1 5.7 %collective-permute-done.8 = f32[32,512]{1,0:T(8,128)S(1)} collective-permute-done((f32[32,512]{1,0:T(8,128)S(1)}, f32[32,512]{1,0:T(8,128)S(1)}, u32[]{:S(2)}, u32[]{:S(2)}) %collective-permute-start.8) | collective-permute-done | bytes 65568 | tf_op jit(solution)/shard_map/ppermute | solution.py:10
  89.4 1.3 collective-permute-start.9
  90.7 5.8 %collective-permute-done.9 = f32[32,512]{1,0:T(8,128)S(1)} collective-permute-done((f32[32,512]{1,0:T(8,128)S(1)}, f32[32,512]{1,0:T(8,128)S(1)}, u32[]{:S(2)}, u32[]{:S(2)}) %collective-permute-start.9) | collective-permute-done | bytes 65568 | tf_op jit(solution)/shard_map/ppermute | solution.py:10
  97.1 1.3 collective-permute-start.10
  98.4 5.8 %collective-permute-done.10 = f32[32,512]{1,0:T(8,128)S(1)} collective-permute-done((f32[32,512]{1,0:T(8,128)S(1)}, f32[32,512]{1,0:T(8,128)S(1)}, u32[]{:S(2)}, u32[]{:S(2)}) %collective-permute-start.10) | collective-permute-done | bytes 65568 | tf_op jit(solution)/shard_map/ppermute | solution.py:10
  104.8 1.3 collective-permute-start.11
  106.1 5.4 %collective-permute-start.6 = (f32[32,512]{1,0:T(8,128)S(1)}, f32[32,512]{1,0:T(8,128)S(1)}, u32[]{:S(2)}, u32[]{:S(2)}) collective-permute-start(f32[32,512]{1,0:T(8,128)S(1)} %get-tuple-element.82), channel_id=1, source_target_pairs={{0,4},{4,8},{8,12},{12,16},{16,20},{20,24},{24,28},{1,5},{5,9},{9,... | collective-permute-start | bytes 196616 | tf_op jit(solution)/shard_map/ppermute | solution.py:10
  111.6 0.3 collective-permute-done.11
  112.5 1.3 collective-permute-start.12
  114.1 5.5 %collective-permute-done.12 = f32[32,512]{1,0:T(8,128)S(1)} collective-permute-done((f32[32,512]{1,0:T(8,128)S(1)}, f32[32,512]{1,0:T(8,128)S(1)}, u32[]{:S(2)}, u32[]{:S(2)}) %collective-permute-start.12) | collective-permute-done | bytes 65568 | tf_op jit(solution)/shard_map/ppermute | solution.py:10
  120.2 1.3 collective-permute-start.13
  121.7 5.5 %collective-permute-done.13 = f32[32,512]{1,0:T(8,128)S(1)} collective-permute-done((f32[32,512]{1,0:T(8,128)S(1)}, f32[32,512]{1,0:T(8,128)S(1)}, u32[]{:S(2)}, u32[]{:S(2)}) %collective-permute-start.13) | collective-permute-done | bytes 65568 | tf_op jit(solution)/shard_map/ppermute | solution.py:10
  127.9 0.7 copy.12
  128.7 1.1 reshape.17
  129.7 8.4 %all_to_all.24 = f32[4,1,16384]{2,1,0:T(1,128)S(1)} all-to-all(f32[4,1,16384]{2,1,0:T(1,128)S(1)} %reshape.17), channel_id=1, replica_groups=mesh['tm'=8,'col'=4] {'col'}, dimensions={0} | all-to-all | bytes 524288 | tf_op jit(solution)/shard_map/all_to_all | solution.py:80
  138.1 0.5 broadcast.3
  138.6 1.4 reduce
  140.0 0.9 reshape.18
  140.9 0.4 fusion.248
  141.3 0.8 copy.13
  142.2 0.8 copy.14
  (91 shorter events, 8.3 us)
Async XLA Ops:
  7.2 0.8 copy-start
  7.2 21.9 %all-gather.2.cloned.1.call-start = ((), (), s32[]{:S(2)}) async-start(), calls=%async_computation.2 | async-start | bytes 1310720 | tf_op jit(solution)/shard_map/all_gather | solution.py:31
  8.7 11.7 %all-to-all-start = ((bf16[2,128,128]{2,0,1:T(2,128)(2,1)}), bf16[2,128,128]{2,0,1:T(2,128)(2,1)S(1)}, u32[]{:S(2)}, u32[]{:S(2)}) async-start(bf16[2,128,128]{2,0,1:T(2,128)(2,1)} %copy.10), calls=%async_computation | async-start | bytes 131072 | tf_op jit(solution)/shard_map/all_to_all | solution.py:36
  12.9 0.7 copy-start.2
  12.9 0.7 copy-start.3
  18.9 0.7 copy-start.1
  30.9 5.3 %collective-permute-start = (f32[32,512]{1,0:T(8,128)S(1)}, f32[32,512]{1,0:T(8,128)S(1)}, u32[]{:S(2)}, u32[]{:S(2)}) collective-permute-start(f32[32,512]{1,0:T(8,128)S(1)} %fusion.53), channel_id=1, source_target_pairs={{0,4},{4,8},{8,12},{12,16},{16,20},{20,24},{24,28},{1,5},{5,9},{9,... | collective-permute-start | bytes 196616 | tf_op jit(solution)/shard_map/ppermute | solution.py:10
  36.7 6.2 %collective-permute-start.1 = (f32[32,512]{1,0:T(8,128)S(1)}, f32[32,512]{1,0:T(8,128)S(1)}, u32[]{:S(2)}, u32[]{:S(2)}) collective-permute-start(f32[32,512]{1,0:T(8,128)S(1)} %fusion.49), channel_id=1, source_target_pairs={{0,4},{4,8},{8,12},{12,16},{16,20},{20,24},{24,28},{1,5},{5,9},{9,... | collective-permute-start | bytes 196616 | tf_op jit(solution)/shard_map/ppermute | solution.py:10
  43.3 6.2 %collective-permute-start.2 = (f32[32,512]{1,0:T(8,128)S(1)}, f32[32,512]{1,0:T(8,128)S(1)}, u32[]{:S(2)}, u32[]{:S(2)}) collective-permute-start(f32[32,512]{1,0:T(8,128)S(1)} %fusion.45), channel_id=1, source_target_pairs={{0,4},{4,8},{8,12},{12,16},{16,20},{20,24},{24,28},{1,5},{5,9},{9,... | collective-permute-start | bytes 196616 | tf_op jit(solution)/shard_map/ppermute | solution.py:10
  50.0 7.1 %collective-permute-start.3 = (f32[32,512]{1,0:T(8,128)S(1)}, f32[32,512]{1,0:T(8,128)S(1)}, u32[]{:S(2)}, u32[]{:S(2)}) collective-permute-start(f32[32,512]{1,0:T(8,128)S(1)} %fusion.41), channel_id=1, source_target_pairs={{0,4},{4,8},{8,12},{12,16},{16,20},{20,24},{24,28},{1,5},{5,9},{9,... | collective-permute-start | bytes 196616 | tf_op jit(solution)/shard_map/ppermute | solution.py:10
  57.5 7.1 %collective-permute-start.4 = (f32[32,512]{1,0:T(8,128)S(1)}, f32[32,512]{1,0:T(8,128)S(1)}, u32[]{:S(2)}, u32[]{:S(2)}) collective-permute-start(f32[32,512]{1,0:T(8,128)S(1)} %fusion.37), channel_id=1, source_target_pairs={{0,4},{4,8},{8,12},{12,16},{16,20},{20,24},{24,28},{1,5},{5,9},{9,... | collective-permute-start | bytes 196616 | tf_op jit(solution)/shard_map/ppermute | solution.py:10
  65.1 7.1 %collective-permute-start.5 = (f32[32,512]{1,0:T(8,128)S(1)}, f32[32,512]{1,0:T(8,128)S(1)}, u32[]{:S(2)}, u32[]{:S(2)}) collective-permute-start(f32[32,512]{1,0:T(8,128)S(1)} %fusion.33), channel_id=1, source_target_pairs={{0,4},{4,8},{8,12},{12,16},{16,20},{20,24},{24,28},{1,5},{5,9},{9,... | collective-permute-start | bytes 196616 | tf_op jit(solution)/shard_map/ppermute | solution.py:10
  73.2 7.9 %collective-permute-start.7 = (f32[32,512]{1,0:T(8,128)S(1)}, f32[32,512]{1,0:T(8,128)S(1)}, u32[]{:S(2)}, u32[]{:S(2)}) collective-permute-start(f32[32,512]{1,0:T(8,128)S(1)} %fusion.21), channel_id=1, source_target_pairs={{4,0},{8,4},{12,8},{16,12},{20,16},{24,20},{28,24},{5,1},{9,5},{13... | collective-permute-start | bytes 196616 | tf_op jit(solution)/shard_map/ppermute | solution.py:10
  81.8 7.0 %collective-permute-start.8 = (f32[32,512]{1,0:T(8,128)S(1)}, f32[32,512]{1,0:T(8,128)S(1)}, u32[]{:S(2)}, u32[]{:S(2)}) collective-permute-start(f32[32,512]{1,0:T(8,128)S(1)} %fusion.18), channel_id=1, source_target_pairs={{4,0},{8,4},{12,8},{16,12},{20,16},{24,20},{28,24},{5,1},{9,5},{13... | collective-permute-start | bytes 196616 | tf_op jit(solution)/shard_map/ppermute | solution.py:10
  89.4 7.1 %collective-permute-start.9 = (f32[32,512]{1,0:T(8,128)S(1)}, f32[32,512]{1,0:T(8,128)S(1)}, u32[]{:S(2)}, u32[]{:S(2)}) collective-permute-start(f32[32,512]{1,0:T(8,128)S(1)} %fusion.15), channel_id=1, source_target_pairs={{4,0},{8,4},{12,8},{16,12},{20,16},{24,20},{28,24},{5,1},{9,5},{13... | collective-permute-start | bytes 196616 | tf_op jit(solution)/shard_map/ppermute | solution.py:10
  97.1 7.1 %collective-permute-start.10 = (f32[32,512]{1,0:T(8,128)S(1)}, f32[32,512]{1,0:T(8,128)S(1)}, u32[]{:S(2)}, u32[]{:S(2)}) collective-permute-start(f32[32,512]{1,0:T(8,128)S(1)} %fusion.12), channel_id=1, source_target_pairs={{4,0},{8,4},{12,8},{16,12},{20,16},{24,20},{28,24},{5,1},{9,5},{13... | collective-permute-start | bytes 196616 | tf_op jit(solution)/shard_map/ppermute | solution.py:10
  104.8 7.1 %collective-permute-start.11 = (f32[32,512]{1,0:T(8,128)S(1)}, f32[32,512]{1,0:T(8,128)S(1)}, u32[]{:S(2)}, u32[]{:S(2)}) collective-permute-start(f32[32,512]{1,0:T(8,128)S(1)} %fusion.9), channel_id=1, source_target_pairs={{4,0},{8,4},{12,8},{16,12},{20,16},{24,20},{28,24},{5,1},{9,5},{13... | collective-permute-start | bytes 196616 | tf_op jit(solution)/shard_map/ppermute | solution.py:10
  106.1 7.9 %collective-permute-start.6 = (f32[32,512]{1,0:T(8,128)S(1)}, f32[32,512]{1,0:T(8,128)S(1)}, u32[]{:S(2)}, u32[]{:S(2)}) collective-permute-start(f32[32,512]{1,0:T(8,128)S(1)} %get-tuple-element.82), channel_id=1, source_target_pairs={{0,4},{4,8},{8,12},{12,16},{16,20},{20,24},{24,28},{1,5},{5,9},{9,... | collective-permute-start | bytes 196616 | tf_op jit(solution)/shard_map/ppermute | solution.py:10
  112.5 7.1 %collective-permute-start.12 = (f32[32,512]{1,0:T(8,128)S(1)}, f32[32,512]{1,0:T(8,128)S(1)}, u32[]{:S(2)}, u32[]{:S(2)}) collective-permute-start(f32[32,512]{1,0:T(8,128)S(1)} %fusion.6), channel_id=1, source_target_pairs={{4,0},{8,4},{12,8},{16,12},{20,16},{24,20},{28,24},{5,1},{9,5},{13... | collective-permute-start | bytes 196616 | tf_op jit(solution)/shard_map/ppermute | solution.py:10
  120.2 7.1 %collective-permute-start.13 = (f32[32,512]{1,0:T(8,128)S(1)}, f32[32,512]{1,0:T(8,128)S(1)}, u32[]{:S(2)}, u32[]{:S(2)}) collective-permute-start(f32[32,512]{1,0:T(8,128)S(1)} %fusion.3), channel_id=1, source_target_pairs={{4,0},{8,4},{12,8},{16,12},{20,16},{24,20},{28,24},{5,1},{9,5},{13... | collective-permute-start | bytes 196616 | tf_op jit(solution)/shard_map/ppermute | solution.py:10
Sparse Core Ops, SparseCore 0:
  9.5 19.5 all-gather.1
where the time goes:
time: 151 us; the launch traced here: 150 us
  waiting for transfers between devices  55.9 us (37%)
  starting transfers between devices  46.2 us (31%)
  between operations  14.6 us (10%)
  blocking collectives  13.7 us (9%)
  local copies, waits for them, and re-layouts  8.34 us (6%)
  matrix products  7.36 us (5%)
  other arithmetic  3.76 us (2%)
    ppermute x14, waiting for transfers between devices, passed_along(): return lax.ppermute(shard, axis, pairs)  46.7 us
    ppermute x14, starting transfers between devices, passed_along(): return lax.ppermute(shard, axis, pairs)  41.9 us
    all_gather x1, waiting for transfers between devices, local(): full_coupling = lax.all_gather(coupling, 'col', axis=2, tiled=True)  8.51 us
    all_to_all x1, blocking collectives, local(): both = lax.all_to_all(both, 'col', split_axis=3, concat_axis=2, tiled=True)  8.39 us
    dot_general x31, matrix products, split_dot(): lax.dot_general(both, weights, (((1,), (contract,)), ((), ())), preferred...  7.36 us
    all_gather x1, blocking collectives, local(): small = lax.all_gather(small, 'col', axis=1, tiled=True)  5.29 us
    all_to_all x1, starting transfers between devices, local(): lax.all_to_all(observed, 'col', split_axis=1, concat_axis=2, tiled=True)  4.24 us
    unnamed x11, local copies, waits for them, and re-layouts  4.14 us
  transfers between devices with their start and end apart: 16, of which 15 were waited for; matrix products, arithmetic and copies ran while one was open for 2% of the time, Pallas kernels for 0%

commit v1 on v0

--- a/solution.py
+++ b/solution.py
@@ -28,7 +28,14 @@
     block_count = pattern.shape[0]
     block_size = state_width // block_count
     time_groups = lax.axis_size("tm")
-    full_coupling = lax.all_gather(coupling, "col", axis=2, tiled=True)
+    x_2 = coupling
+    ways, here, lap = (lax.axis_size("col"), lax.axis_index("col"), x_2.shape[2])
+    shape = [n * ways if d == 2 else n for d, n in enumerate(x_2.shape)]
+    full = lax.dynamic_update_slice_in_dim(jnp.zeros(shape, x_2.dtype), x_2, here * lap, axis=2)
+    for far in range(1, ways):
+        x_2 = lax.ppermute(x_2, "col", [(d, (d + 1) % ways) for d in range(ways)])
+        full = lax.dynamic_update_slice_in_dim(full, x_2, (here - far) % ways * lap, axis=2)
+    full_coupling = full
     small = jnp.concatenate([persist, input_gain[None]], axis=0)
     small = lax.all_gather(small, "col", axis=1, tiled=True)
     diag = small[:step_count]

time: 151 us -> 140 us (0.927)
  between operations: 14.6 us -> 1.33 us
  local copies, waits for them, and re-layouts: 8.34 us -> 10.3 us
    ppermute x0 -> x3, waiting for transfers between devices: none -> 8.51 us  [local(): x_2 = lax.ppermute(x_2, 'col', [(d, (d + 1) % ways) for d in range(ways)])]
    all_gather x1 -> x0, waiting for transfers between devices: 8.51 us -> none  [local(): full_coupling = lax.all_gather(coupling, 'col', axis=2, tiled=True)]
    unnamed x11, local copies, waits for them, and re-layouts: 4.14 us -> 5.75 us
  transfers between devices with their start and end apart: 16 -> 18, of which waited for: 15 -> 15; matrix products, arithmetic and copies ran while one was open for 2% -> 3% of each run, Pallas kernels for 0% -> 0%
where the time goes in v1:
time: 140 us; the launch traced here: 139 us
  waiting for transfers between devices  55.3 us (40%)
  starting transfers between devices  46.9 us (34%)
  blocking collectives  15.1 us (11%)
  local copies, waits for them, and re-layouts  10.3 us (7%)
  matrix products  7.33 us (5%)
  other arithmetic  2.53 us (2%)
    ppermute x14, waiting for transfers between devices, passed_along(): return lax.ppermute(shard, axis, pairs)  46.8 us
    ppermute x14, starting transfers between devices, passed_along(): return lax.ppermute(shard, axis, pairs)  42.3 us
    all_to_all x1, blocking collectives, local(): both = lax.all_to_all(both, 'col', split_axis=3, concat_axis=2, tiled=True)  9.18 us
    ppermute x3, waiting for transfers between devices, local(): x_2 = lax.ppermute(x_2, 'col', [(d, (d + 1) % ways) for d in range(ways)])  8.51 us
    dot_general x31, matrix products, split_dot(): lax.dot_general(both, weights, (((1,), (contract,)), ((), ())), preferred...  7.33 us
    all_gather x1, blocking collectives, local(): small = lax.all_gather(small, 'col', axis=1, tiled=True)  5.89 us
    unnamed x11, local copies, waits for them, and re-layouts  5.75 us
    all_to_all x1, starting transfers between devices, local(): lax.all_to_all(observed, 'col', split_axis=1, concat_axis=2, tiled=True)  3.86 us
  transfers between devices with their start and end apart: 18, of which 15 were waited for; matrix products, arithmetic and copies ran while one was open for 3% of the time, Pallas kernels for 0%

profile of v1, /device:TPU:0, one launch (start us, length us, event | category | flops | bytes accessed | tf_op | source)
XLA Modules:
  0.0 138.8 jit_solution(16682823817032455229)
XLA Ops:
  0.6 0.5 collective-permute-start
  1.2 1.5 %copy.10 = bf16[2,128,128]{2,0,1:T(2,128)(2,1)} copy(bf16[2,128,128]{2,1,0:T(8,128)(2,1)} %param.5) | data formatting | bytes 131072 | tf_op args[0]
  2.7 3.9 %all-to-all-start = ((bf16[2,128,128]{2,0,1:T(2,128)(2,1)}), bf16[2,128,128]{2,0,1:T(2,128)(2,1)S(1)}, u32[]{:S(2)}, u32[]{:S(2)}) async-start(bf16[2,128,128]{2,0,1:T(2,128)(2,1)} %copy.10), calls=%async_computation | async-start | bytes 131072 | tf_op jit(solution)/shard_map/all_to_all | solution.py:43
  6.6 0.7 copy-done.2
  7.3 5.9 %all_gather.3 = f32[3,512]{1,0:T(4,128)S(1)} all-gather(f32[3,128]{1,0:T(4,128)S(1)} %pad_maximum_fusion.1), channel_id=1, replica_groups=mesh['tm'=8,'col'=4] {'col'}, dimensions={1}, use_global_device_ids=true | all-gather | bytes 7680 | tf_op jit(solution)/shard_map/all_gather | solution.py:40
  13.5 0.9 copy-done
  14.5 0.7 copy-done.1
  15.4 0.6 mul.94
  16.1 2.9 %collective-permute-done.1 = bf16[2,512,128]{2,1,0:T(8,128)(2,1)S(1)} collective-permute-done((bf16[2,512,128]{2,1,0:T(8,128)(2,1)S(1)}, bf16[2,512,128]{2,1,0:T(8,128)(2,1)S(1)}, u32[]{:S(2)}, u32[]{:S(2)}) %collective-permute-start.1) | collective-permute-done | bytes 262176 | tf_op jit(solution)/shard_map/ppermute | solution.py:36
  19.2 5.6 %collective-permute-done.2 = bf16[2,512,128]{2,1,0:T(8,128)(2,1)S(1)} collective-permute-done((bf16[2,512,128]{2,1,0:T(8,128)(2,1)S(1)}, bf16[2,512,128]{2,1,0:T(8,128)(2,1)S(1)}, u32[]{:S(2)}, u32[]{:S(2)}) %collective-permute-start.2) | collective-permute-done | bytes 262176 | tf_op jit(solution)/shard_map/ppermute | solution.py:36
  25.5 3.4 %collective-permute-start.3 = (f32[32,512]{1,0:T(8,128)S(1)}, f32[32,512]{1,0:T(8,128)S(1)}, u32[]{:S(2)}, u32[]{:S(2)}) collective-permute-start(f32[32,512]{1,0:T(8,128)S(1)} %fusion.53), channel_id=1, source_target_pairs={{0,4},{4,8},{8,12},{12,16},{16,20},{20,24},{24,28},{1,5},{5,9},{9,... | collective-permute-start | bytes 196616 | tf_op jit(solution)/shard_map/ppermute | solution.py:10
  28.9 1.9 %collective-permute-done.3 = f32[32,512]{1,0:T(8,128)S(1)} collective-permute-done((f32[32,512]{1,0:T(8,128)S(1)}, f32[32,512]{1,0:T(8,128)S(1)}, u32[]{:S(2)}, u32[]{:S(2)}) %collective-permute-start.3) | collective-permute-done | bytes 65568 | tf_op jit(solution)/shard_map/ppermute | solution.py:10
  31.3 4.3 %collective-permute-start.4 = (f32[32,512]{1,0:T(8,128)S(1)}, f32[32,512]{1,0:T(8,128)S(1)}, u32[]{:S(2)}, u32[]{:S(2)}) collective-permute-start(f32[32,512]{1,0:T(8,128)S(1)} %fusion.49), channel_id=1, source_target_pairs={{0,4},{4,8},{8,12},{12,16},{16,20},{20,24},{24,28},{1,5},{5,9},{9,... | collective-permute-start | bytes 196616 | tf_op jit(solution)/shard_map/ppermute | solution.py:10
  35.5 1.9 %collective-permute-done.4 = f32[32,512]{1,0:T(8,128)S(1)} collective-permute-done((f32[32,512]{1,0:T(8,128)S(1)}, f32[32,512]{1,0:T(8,128)S(1)}, u32[]{:S(2)}, u32[]{:S(2)}) %collective-permute-start.4) | collective-permute-done | bytes 65568 | tf_op jit(solution)/shard_map/ppermute | solution.py:10
  37.9 4.3 %collective-permute-start.5 = (f32[32,512]{1,0:T(8,128)S(1)}, f32[32,512]{1,0:T(8,128)S(1)}, u32[]{:S(2)}, u32[]{:S(2)}) collective-permute-start(f32[32,512]{1,0:T(8,128)S(1)} %fusion.45), channel_id=1, source_target_pairs={{0,4},{4,8},{8,12},{12,16},{16,20},{20,24},{24,28},{1,5},{5,9},{9,... | collective-permute-start | bytes 196616 | tf_op jit(solution)/shard_map/ppermute | solution.py:10
  42.2 1.9 %collective-permute-done.5 = f32[32,512]{1,0:T(8,128)S(1)} collective-permute-done((f32[32,512]{1,0:T(8,128)S(1)}, f32[32,512]{1,0:T(8,128)S(1)}, u32[]{:S(2)}, u32[]{:S(2)}) %collective-permute-start.5) | collective-permute-done | bytes 65568 | tf_op jit(solution)/shard_map/ppermute | solution.py:10
  44.6 5.2 %collective-permute-start.6 = (f32[32,512]{1,0:T(8,128)S(1)}, f32[32,512]{1,0:T(8,128)S(1)}, u32[]{:S(2)}, u32[]{:S(2)}) collective-permute-start(f32[32,512]{1,0:T(8,128)S(1)} %fusion.41), channel_id=1, source_target_pairs={{0,4},{4,8},{8,12},{12,16},{16,20},{20,24},{24,28},{1,5},{5,9},{9,... | collective-permute-start | bytes 196616 | tf_op jit(solution)/shard_map/ppermute | solution.py:10
  49.8 1.9 %collective-permute-done.6 = f32[32,512]{1,0:T(8,128)S(1)} collective-permute-done((f32[32,512]{1,0:T(8,128)S(1)}, f32[32,512]{1,0:T(8,128)S(1)}, u32[]{:S(2)}, u32[]{:S(2)}) %collective-permute-start.6) | collective-permute-done | bytes 65568 | tf_op jit(solution)/shard_map/ppermute | solution.py:10
  52.2 5.2 %collective-permute-start.7 = (f32[32,512]{1,0:T(8,128)S(1)}, f32[32,512]{1,0:T(8,128)S(1)}, u32[]{:S(2)}, u32[]{:S(2)}) collective-permute-start(f32[32,512]{1,0:T(8,128)S(1)} %fusion.37), channel_id=1, source_target_pairs={{0,4},{4,8},{8,12},{12,16},{16,20},{20,24},{24,28},{1,5},{5,9},{9,... | collective-permute-start | bytes 196616 | tf_op jit(solution)/shard_map/ppermute | solution.py:10
  57.3 2.0 %collective-permute-done.7 = f32[32,512]{1,0:T(8,128)S(1)} collective-permute-done((f32[32,512]{1,0:T(8,128)S(1)}, f32[32,512]{1,0:T(8,128)S(1)}, u32[]{:S(2)}, u32[]{:S(2)}) %collective-permute-start.7) | collective-permute-done | bytes 65568 | tf_op jit(solution)/shard_map/ppermute | solution.py:10
  59.8 5.5 %collective-permute-start.8 = (f32[32,512]{1,0:T(8,128)S(1)}, f32[32,512]{1,0:T(8,128)S(1)}, u32[]{:S(2)}, u32[]{:S(2)}) collective-permute-start(f32[32,512]{1,0:T(8,128)S(1)} %fusion.33), channel_id=1, source_target_pairs={{0,4},{4,8},{8,12},{12,16},{16,20},{20,24},{24,28},{1,5},{5,9},{9,... | collective-permute-start | bytes 196616 | tf_op jit(solution)/shard_map/ppermute | solution.py:10
  65.3 1.9 %collective-permute-done.8 = f32[32,512]{1,0:T(8,128)S(1)} collective-permute-done((f32[32,512]{1,0:T(8,128)S(1)}, f32[32,512]{1,0:T(8,128)S(1)}, u32[]{:S(2)}, u32[]{:S(2)}) %collective-permute-start.8) | collective-permute-done | bytes 65568 | tf_op jit(solution)/shard_map/ppermute | solution.py:10
  68.3 1.3 collective-permute-start.10
  69.6 6.2 %collective-permute-done.10 = f32[32,512]{1,0:T(8,128)S(1)} collective-permute-done((f32[32,512]{1,0:T(8,128)S(1)}, f32[32,512]{1,0:T(8,128)S(1)}, u32[]{:S(2)}, u32[]{:S(2)}) %collective-permute-start.10) | collective-permute-done | bytes 65568 | tf_op jit(solution)/shard_map/ppermute | solution.py:10
  76.4 1.3 collective-permute-start.11
  77.7 6.1 %collective-permute-done.11 = f32[32,512]{1,0:T(8,128)S(1)} collective-permute-done((f32[32,512]{1,0:T(8,128)S(1)}, f32[32,512]{1,0:T(8,128)S(1)}, u32[]{:S(2)}, u32[]{:S(2)}) %collective-permute-start.11) | collective-permute-done | bytes 65568 | tf_op jit(solution)/shard_map/ppermute | solution.py:10
  84.2 0.3 fusion.136
  84.5 1.3 collective-permute-start.12
  85.8 5.8 %collective-permute-done.12 = f32[32,512]{1,0:T(8,128)S(1)} collective-permute-done((f32[32,512]{1,0:T(8,128)S(1)}, f32[32,512]{1,0:T(8,128)S(1)}, u32[]{:S(2)}, u32[]{:S(2)}) %collective-permute-start.12) | collective-permute-done | bytes 65568 | tf_op jit(solution)/shard_map/ppermute | solution.py:10
  91.5 0.3 fusion.140
  92.2 1.3 collective-permute-start.13
  93.5 5.8 %collective-permute-done.13 = f32[32,512]{1,0:T(8,128)S(1)} collective-permute-done((f32[32,512]{1,0:T(8,128)S(1)}, f32[32,512]{1,0:T(8,128)S(1)}, u32[]{:S(2)}, u32[]{:S(2)}) %collective-permute-start.13) | collective-permute-done | bytes 65568 | tf_op jit(solution)/shard_map/ppermute | solution.py:10
  99.9 1.3 collective-permute-start.14
  101.2 5.4 %collective-permute-start.9 = (f32[32,512]{1,0:T(8,128)S(1)}, f32[32,512]{1,0:T(8,128)S(1)}, u32[]{:S(2)}, u32[]{:S(2)}) collective-permute-start(f32[32,512]{1,0:T(8,128)S(1)} %get-tuple-element.82), channel_id=1, source_target_pairs={{0,4},{4,8},{8,12},{12,16},{16,20},{20,24},{24,28},{1,5},{5,9},{9,... | collective-permute-start | bytes 196616 | tf_op jit(solution)/shard_map/ppermute | solution.py:10
  106.6 0.3 collective-permute-done.14
  107.6 1.3 collective-permute-start.15
  108.9 5.7 %collective-permute-done.15 = f32[32,512]{1,0:T(8,128)S(1)} collective-permute-done((f32[32,512]{1,0:T(8,128)S(1)}, f32[32,512]{1,0:T(8,128)S(1)}, u32[]{:S(2)}, u32[]{:S(2)}) %collective-permute-start.15) | collective-permute-done | bytes 65568 | tf_op jit(solution)/shard_map/ppermute | solution.py:10
  115.3 1.3 collective-permute-start.16
  116.8 5.5 %collective-permute-done.16 = f32[32,512]{1,0:T(8,128)S(1)} collective-permute-done((f32[32,512]{1,0:T(8,128)S(1)}, f32[32,512]{1,0:T(8,128)S(1)}, u32[]{:S(2)}, u32[]{:S(2)}) %collective-permute-start.16) | collective-permute-done | bytes 65568 | tf_op jit(solution)/shard_map/ppermute | solution.py:10
  123.0 0.7 copy.12
  123.7 1.0 reshape.17
  124.7 9.2 %all_to_all.24 = f32[4,1,16384]{2,1,0:T(1,128)S(1)} all-to-all(f32[4,1,16384]{2,1,0:T(1,128)S(1)} %reshape.17), channel_id=1, replica_groups=mesh['tm'=8,'col'=4] {'col'}, dimensions={0} | all-to-all | bytes 524288 | tf_op jit(solution)/shard_map/all_to_all | solution.py:87
  133.9 0.5 broadcast.6
  134.4 1.4 reduce
  135.8 0.9 reshape.18
  136.7 0.4 fusion.248
  137.1 0.8 copy.13
  138.0 0.8 copy.14
  (99 shorter events, 8.8 us)
Async XLA Ops:
  0.6 12.5 %collective-permute-start = (bf16[2,512,128]{2,1,0:T(8,128)(2,1)}, bf16[2,512,128]{2,1,0:T(8,128)(2,1)S(1)}, u32[]{:S(2)}, u32[]{:S(2)}) collective-permute-start(bf16[2,512,128]{2,1,0:T(8,128)(2,1)} %param.8), channel_id=1, source_target_pairs={{0,1},{1,2},{2,3},{3,0},{4,5},{5,6},{6,7},{7,4},{8,9},{9,10},{10,1... | collective-permute-start | bytes 786440 | tf_op jit(solution)/shard_map/ppermute | solution.py:36
  2.7 13.3 %all-to-all-start = ((bf16[2,128,128]{2,0,1:T(2,128)(2,1)}), bf16[2,128,128]{2,0,1:T(2,128)(2,1)S(1)}, u32[]{:S(2)}, u32[]{:S(2)}) async-start(bf16[2,128,128]{2,0,1:T(2,128)(2,1)} %copy.10), calls=%async_computation | async-start | bytes 131072 | tf_op jit(solution)/shard_map/all_to_all | solution.py:43
  6.6 0.7 copy-start.2
  6.6 0.7 copy-start.3
  13.2 5.8 %collective-permute-start.1 = (bf16[2,512,128]{2,1,0:T(8,128)(2,1)S(1)}, bf16[2,512,128]{2,1,0:T(8,128)(2,1)S(1)}, u32[]{:S(2)}, u32[]{:S(2)}) collective-permute-start(bf16[2,512,128]{2,1,0:T(8,128)(2,1)S(1)} %collective-permute-done), channel_id=1, source_target_pairs={{0,1},{1,2},{2,3},{3,0},{4,5},{5,6},{6,7},{7,4},{8,9},{9,10},{10,1... | collective-permute-start | bytes 786440 | tf_op jit(solution)/shard_map/ppermute | solution.py:36
  13.4 0.9 copy-start
  14.5 0.7 copy-start.1
  19.0 5.8 %collective-permute-start.2 = (bf16[2,512,128]{2,1,0:T(8,128)(2,1)S(1)}, bf16[2,512,128]{2,1,0:T(8,128)(2,1)S(1)}, u32[]{:S(2)}, u32[]{:S(2)}) collective-permute-start(bf16[2,512,128]{2,1,0:T(8,128)(2,1)S(1)} %collective-permute-done.1), channel_id=1, source_target_pairs={{0,1},{1,2},{2,3},{3,0},{4,5},{5,6},{6,7},{7,4},{8,9},{9,10},{10,1... | collective-permute-start | bytes 786440 | tf_op jit(solution)/shard_map/ppermute | solution.py:36
  25.5 5.3 %collective-permute-start.3 = (f32[32,512]{1,0:T(8,128)S(1)}, f32[32,512]{1,0:T(8,128)S(1)}, u32[]{:S(2)}, u32[]{:S(2)}) collective-permute-start(f32[32,512]{1,0:T(8,128)S(1)} %fusion.53), channel_id=1, source_target_pairs={{0,4},{4,8},{8,12},{12,16},{16,20},{20,24},{24,28},{1,5},{5,9},{9,... | collective-permute-start | bytes 196616 | tf_op jit(solution)/shard_map/ppermute | solution.py:10
  31.3 6.2 %collective-permute-start.4 = (f32[32,512]{1,0:T(8,128)S(1)}, f32[32,512]{1,0:T(8,128)S(1)}, u32[]{:S(2)}, u32[]{:S(2)}) collective-permute-start(f32[32,512]{1,0:T(8,128)S(1)} %fusion.49), channel_id=1, source_target_pairs={{0,4},{4,8},{8,12},{12,16},{16,20},{20,24},{24,28},{1,5},{5,9},{9,... | collective-permute-start | bytes 196616 | tf_op jit(solution)/shard_map/ppermute | solution.py:10
  37.9 6.2 %collective-permute-start.5 = (f32[32,512]{1,0:T(8,128)S(1)}, f32[32,512]{1,0:T(8,128)S(1)}, u32[]{:S(2)}, u32[]{:S(2)}) collective-permute-start(f32[32,512]{1,0:T(8,128)S(1)} %fusion.45), channel_id=1, source_target_pairs={{0,4},{4,8},{8,12},{12,16},{16,20},{20,24},{24,28},{1,5},{5,9},{9,... | collective-permute-start | bytes 196616 | tf_op jit(solution)/shard_map/ppermute | solution.py:10
  44.6 7.1 %collective-permute-start.6 = (f32[32,512]{1,0:T(8,128)S(1)}, f32[32,512]{1,0:T(8,128)S(1)}, u32[]{:S(2)}, u32[]{:S(2)}) collective-permute-start(f32[32,512]{1,0:T(8,128)S(1)} %fusion.41), channel_id=1, source_target_pairs={{0,4},{4,8},{8,12},{12,16},{16,20},{20,24},{24,28},{1,5},{5,9},{9,... | collective-permute-start | bytes 196616 | tf_op jit(solution)/shard_map/ppermute | solution.py:10
  52.2 7.2 %collective-permute-start.7 = (f32[32,512]{1,0:T(8,128)S(1)}, f32[32,512]{1,0:T(8,128)S(1)}, u32[]{:S(2)}, u32[]{:S(2)}) collective-permute-start(f32[32,512]{1,0:T(8,128)S(1)} %fusion.37), channel_id=1, source_target_pairs={{0,4},{4,8},{8,12},{12,16},{16,20},{20,24},{24,28},{1,5},{5,9},{9,... | collective-permute-start | bytes 196616 | tf_op jit(solution)/shard_map/ppermute | solution.py:10
  59.8 7.4 %collective-permute-start.8 = (f32[32,512]{1,0:T(8,128)S(1)}, f32[32,512]{1,0:T(8,128)S(1)}, u32[]{:S(2)}, u32[]{:S(2)}) collective-permute-start(f32[32,512]{1,0:T(8,128)S(1)} %fusion.33), channel_id=1, source_target_pairs={{0,4},{4,8},{8,12},{12,16},{16,20},{20,24},{24,28},{1,5},{5,9},{9,... | collective-permute-start | bytes 196616 | tf_op jit(solution)/shard_map/ppermute | solution.py:10
  68.3 7.5 %collective-permute-start.10 = (f32[32,512]{1,0:T(8,128)S(1)}, f32[32,512]{1,0:T(8,128)S(1)}, u32[]{:S(2)}, u32[]{:S(2)}) collective-permute-start(f32[32,512]{1,0:T(8,128)S(1)} %fusion.21), channel_id=1, source_target_pairs={{4,0},{8,4},{12,8},{16,12},{20,16},{24,20},{28,24},{5,1},{9,5},{13... | collective-permute-start | bytes 196616 | tf_op jit(solution)/shard_map/ppermute | solution.py:10
  76.4 7.4 %collective-permute-start.11 = (f32[32,512]{1,0:T(8,128)S(1)}, f32[32,512]{1,0:T(8,128)S(1)}, u32[]{:S(2)}, u32[]{:S(2)}) collective-permute-start(f32[32,512]{1,0:T(8,128)S(1)} %fusion.18), channel_id=1, source_target_pairs={{4,0},{8,4},{12,8},{16,12},{20,16},{24,20},{28,24},{5,1},{9,5},{13... | collective-permute-start | bytes 196616 | tf_op jit(solution)/shard_map/ppermute | solution.py:10
  84.5 7.1 %collective-permute-start.12 = (f32[32,512]{1,0:T(8,128)S(1)}, f32[32,512]{1,0:T(8,128)S(1)}, u32[]{:S(2)}, u32[]{:S(2)}) collective-permute-start(f32[32,512]{1,0:T(8,128)S(1)} %fusion.15), channel_id=1, source_target_pairs={{4,0},{8,4},{12,8},{16,12},{20,16},{24,20},{28,24},{5,1},{9,5},{13... | collective-permute-start | bytes 196616 | tf_op jit(solution)/shard_map/ppermute | solution.py:10
  92.2 7.1 %collective-permute-start.13 = (f32[32,512]{1,0:T(8,128)S(1)}, f32[32,512]{1,0:T(8,128)S(1)}, u32[]{:S(2)}, u32[]{:S(2)}) collective-permute-start(f32[32,512]{1,0:T(8,128)S(1)} %fusion.12), channel_id=1, source_target_pairs={{4,0},{8,4},{12,8},{16,12},{20,16},{24,20},{28,24},{5,1},{9,5},{13... | collective-permute-start | bytes 196616 | tf_op jit(solution)/shard_map/ppermute | solution.py:10
  99.9 7.1 %collective-permute-start.14 = (f32[32,512]{1,0:T(8,128)S(1)}, f32[32,512]{1,0:T(8,128)S(1)}, u32[]{:S(2)}, u32[]{:S(2)}) collective-permute-start(f32[32,512]{1,0:T(8,128)S(1)} %fusion.9), channel_id=1, source_target_pairs={{4,0},{8,4},{12,8},{16,12},{20,16},{24,20},{28,24},{5,1},{9,5},{13... | collective-permute-start | bytes 196616 | tf_op jit(solution)/shard_map/ppermute | solution.py:10
  101.2 7.7 %collective-permute-start.9 = (f32[32,512]{1,0:T(8,128)S(1)}, f32[32,512]{1,0:T(8,128)S(1)}, u32[]{:S(2)}, u32[]{:S(2)}) collective-permute-start(f32[32,512]{1,0:T(8,128)S(1)} %get-tuple-element.82), channel_id=1, source_target_pairs={{0,4},{4,8},{8,12},{12,16},{16,20},{20,24},{24,28},{1,5},{5,9},{9,... | collective-permute-start | bytes 196616 | tf_op jit(solution)/shard_map/ppermute | solution.py:10
  107.6 7.1 %collective-permute-start.15 = (f32[32,512]{1,0:T(8,128)S(1)}, f32[32,512]{1,0:T(8,128)S(1)}, u32[]{:S(2)}, u32[]{:S(2)}) collective-permute-start(f32[32,512]{1,0:T(8,128)S(1)} %fusion.6), channel_id=1, source_target_pairs={{4,0},{8,4},{12,8},{16,12},{20,16},{24,20},{28,24},{5,1},{9,5},{13... | collective-permute-start | bytes 196616 | tf_op jit(solution)/shard_map/ppermute | solution.py:10
  115.3 7.1 %collective-permute-start.16 = (f32[32,512]{1,0:T(8,128)S(1)}, f32[32,512]{1,0:T(8,128)S(1)}, u32[]{:S(2)}, u32[]{:S(2)}) collective-permute-start(f32[32,512]{1,0:T(8,128)S(1)} %fusion.3), channel_id=1, source_target_pairs={{4,0},{8,4},{12,8},{16,12},{20,16},{24,20},{28,24},{5,1},{9,5},{13... | collective-permute-start | bytes 196616 | tf_op jit(solution)/shard_map/ppermute | solution.py:10
